TPU v7x, 32 devices: a whole 2x2x4 slice. The times are simulated.
32 devices in a mesh: groups: 2 (over y), frames: 4 (over z), heads: 4 (over x, core).
Axes of the slice: x: 2, y: 2, z: 4, core: 2. Of those that a mesh axis runs over, the one named last changes fastest.
Arguments:
- query_heads: bfloat16 [16384, 896], P(('groups', 'frames'), 'heads'), parts along dimension 0, may hold values from -6 to 6
- key_heads: bfloat16 [16384, 896], P(('groups', 'frames'), 'heads'), parts along dimension 0, may hold values from -0.04 to 8
- value_heads: bfloat16 [16384, 896], P(('groups', 'frames'), 'heads'), parts along dimension 0, may hold values from -6 to 6
- residual: bfloat16 [16384, 2240], P(('groups', 'frames', 'heads')), parts along dimension 0, may hold values from -6 to 6
- out_proj: bfloat16 [896, 2240], P('frames'), may hold values from -0.1875 to 0.1875
- frame_gate: float32 [32, 2240], P(('groups', 'frames')), parts along dimension 0, may hold values from -4 to 4
Outputs:
- updated: bfloat16 [16384, 2240], P(('groups', 'frames', 'heads')), parts along dimension 0
There are 2 independent parts, one for each index of `groups`. A program takes and returns all parts, laid end to end along the dimension named above; an argument that names none is the same for every part. Nothing has to cross between parts.
All inputs are finite; a program needn't handle non-finite values.
Results may differ from a plain program's by a relative error of at most 0.0033.
Values may be sent and summed in bfloat16 or wider, within the bound.
No kernel may reach another device: no remote copies, remote signals or barrier semaphores. Data moves between devices by JAX's collectives and lax.ppermute only.
A program may use at most 64 MiB of HBM per device.

v0:
```python
import jax
import jax.numpy as jnp
from jax import lax
from jax.sharding import PartitionSpec as P

HD = 112
HEADS_DEV = 2
FRAME_TOK = 512
EPSILON = 1e-06


def per_device(query_heads, key_heads, value_heads, residual, out_proj, frame_gate):
    length = query_heads.shape[0]
    frames_here = length // FRAME_TOK
    block_shape = (frames_here, FRAME_TOK, HEADS_DEV, HD)
    query_pos = jnp.maximum(query_heads, 0).reshape(block_shape)
    key_pos = jnp.maximum(key_heads, 0).reshape(block_shape)
    value_frames = value_heads.reshape(block_shape)
    frame_state = jnp.einsum(
        "fthi,fthj->fhij", key_pos, value_frames, preferred_element_type=jnp.float32
    )
    frame_sum = jnp.sum(key_pos, axis=1, dtype=jnp.float32)
    own_state = jnp.sum(frame_state, axis=0)
    own_sum = jnp.sum(frame_sum, axis=0)
    position = lax.axis_index("frames")
    gathered = (
        lax.all_gather(own_state[None], "frames", axis=0, tiled=True),
        lax.all_gather(own_sum[None], "frames", axis=0, tiled=True),
    )
    pieces = gathered[0].shape[0]
    is_lower = jnp.arange(pieces, dtype=jnp.int32) < position
    state_part = jnp.sum(jnp.where(is_lower[:, None, None, None], gathered[0], 0.0), axis=0)
    sum_part = jnp.sum(jnp.where(is_lower[:, None, None], gathered[1], 0.0), axis=0)
    prefix_state = state_part[None] + jnp.cumsum(frame_state, axis=0)
    prefix_sum = sum_part[None] + jnp.cumsum(frame_sum, axis=0)
    state_round = prefix_state.astype(jnp.bfloat16)
    sum_round = prefix_sum.astype(jnp.bfloat16)
    numerator = jnp.einsum(
        "fthi,fhij->fthj", query_pos, state_round, preferred_element_type=jnp.float32
    )
    denominator = (
        jnp.einsum("fthi,fhi->fth", query_pos, sum_round, preferred_element_type=jnp.float32)
        + EPSILON
    )
    attended = (
        (numerator / denominator[..., None]).astype(jnp.bfloat16).reshape(length, HEADS_DEV * HD)
    )
    rows_here = residual.shape[0]
    head_pos = lax.axis_index("heads")
    row_frame = (head_pos * rows_here + jnp.arange(rows_here, dtype=jnp.int32)) // FRAME_TOK
    selector = (row_frame[:, None] == jnp.arange(frames_here, dtype=jnp.int32)[None, :]).astype(
        jnp.float32
    )
    gate_rows = jnp.dot(
        selector, frame_gate, precision=lax.Precision.HIGHEST, preferred_element_type=jnp.float32
    )
    token_rows = lax.all_to_all(attended, "heads", split_axis=0, concat_axis=1, tiled=True)
    projected = jnp.dot(
        token_rows,
        lax.all_gather(out_proj, "frames", axis=0, tiled=True),
        preferred_element_type=jnp.float32,
    )
    return (residual.astype(jnp.float32) + gate_rows * projected).astype(jnp.bfloat16)


def solution(mesh):
    in_specs = (
        P(("groups", "frames"), "heads"),
        P(("groups", "frames"), "heads"),
        P(("groups", "frames"), "heads"),
        P(("groups", "frames", "heads"), None),
        P("frames", None),
        P(("groups", "frames"), None),
    )
    out_specs = P(("groups", "frames", "heads"), None)
    return jax.shard_map(
        per_device, mesh=mesh, in_specs=in_specs, out_specs=out_specs, check_vma=False
    )
```

profile of v0, /device:TPU:0, one launch (start us, length us, event | category | flops | bytes accessed | tf_op | source)
XLA Modules:
  0.0 113.2 jit_solution(14616134283706953128)
XLA Ops:
  6.5 0.0 copy-start
  6.5 0.0 copy-start.1
  6.5 0.0 all-gather.3.cloned.1.call-start
  6.5 0.7 all-gather.3.cloned.1.call-update
  7.3 1.4 %convert_reduce_fusion.1 = f32[224]{0:T(256)S(1)} fusion(bf16[2048,224]{0,1:T(8,128)(2,1)} %param.7), kind=kLoop, calls=%fused_computation.6 | loop fusion | flops 1376032 | bytes 918400 | tf_op jit(solution)/shard_map/reduce_sum | solution.py:24
  8.7 0.1 broadcast_in_dim.41
  8.8 1.2 %broadcast_maximum_fusion = bf16[2048,224]{0,1:T(8,128)(2,1)S(1)} fusion(bf16[2048,224]{0,1:T(8,128)(2,1)} %param.6), kind=kLoop, calls=%fused_computation.16 | loop fusion | flops 458752 | bytes 1835008 | tf_op jit(solution)/shard_map/max | solution.py:16
  10.0 0.7 reshape.48
  10.7 3.2 %reshape.47 = bf16[4,512,2,112]{1,0,3,2:T(4,128)(2,1)} reshape(bf16[2048,224]{0,1:T(8,128)(2,1)} %param.8) | data formatting | bytes 1835008 | tf_op jit(solution)/shard_map/reshape | solution.py:18
  13.9 0.0 copy-done.1
  13.9 0.1 broadcast_maximum_fusion.1
  14.0 0.7 reshape.46
  14.7 0.4 convert_reduce_fusion
  15.1 0.4 reduce_window_sum.23
  15.5 13.3 %all_gather.10 = f32[4,2,112]{2,1,0:T(2,128)S(1)} all-gather(f32[1,2,112]{2,1,0:T(2,128)S(1)} %broadcast_in_dim.41), channel_id=1, replica_groups=mesh['groups'=2,'frames'=4,'heads'=4] {'frames'}, dimensions={0}, use_global_device_ids=true | all-gather | bytes 4480 | tf_op jit(solution)/shard_map/all_gather | solution.py:28
  28.8 0.1 select_reduce_fusion.1
  28.9 0.1 fusion.12
  29.0 0.1 copy.16
  29.1 1.8 %fusion.17 = (f32[2,112,112]{2,1,0:T(8,128)S(1)}, f32[4,2,112,112]{3,2,1,0:T(8,128)S(1)}) fusion(bf16[4,512,2,112]{1,0,3,2:T(4,128)(2,1)} %reshape.47, bf16[4,512,2,112]{1,0,3,2:T(4,128)(2,1)S(1)} %reshape.46), kind=kOutput, calls=%fused_computation.36 | convolution fusion | flops 102835712 | bytes 2336768 | tf_op jit(solution)/shard_map/fthi,fthj->fhij/dot_general | solution.py:19
  30.9 19.9 %all-gather = f32[8,112,112]{2,1,0:T(8,128)S(1)} all-gather(f32[2,112,112]{2,1,0:T(8,128)S(1)} %get-tuple-element.5), channel_id=2, replica_groups=mesh['groups'=2,'frames'=4,'heads'=4] {'frames'}, dimensions={0}, use_global_device_ids=true | all-gather | bytes 501760 | tf_op jit(solution)/shard_map/all_gather | solution.py:27
  50.8 0.1 select_reduce_fusion
  50.9 0.4 fusion.7
  51.3 0.1 fusion.3
  51.3 1.4 %fusion.2 = bf16[4,512,2,112]{1,3,2,0:T(8,128)(2,1)} fusion(bf16[4,2,112,112]{3,2,1,0:T(8,128)(2,1)S(1)} %fusion.3, f32[4,512,2]{1,2,0:T(2,128)S(1)} %fusion.13, bf16[4,512,2,112]{1,0,3,2:T(4,128)(2,1)S(1)} %reshape.48), kind=kOutput, calls=%fused_computation.4 | convolution fusion | flops 103677952 | bytes 2052096 | tf_op jit(solution)/shard_map/fthi,fhij->fthj/dot_general | solution.py:38
  52.7 0.0 copy-start.2
  52.7 3.6 %all-to-all-start = ((bf16[4,512,224]{1,2,0:T(8,128)(2,1)}), bf16[4,512,224]{1,2,0:T(8,128)(2,1)S(1)}, u32[]{:S(2)}, u32[]{:S(2)}) async-start(bf16[4,512,224]{1,2,0:T(8,128)(2,1)} %bitcast.5), calls=%async_computation | async-start | bytes 1835008 | tf_op jit(solution)/shard_map/all_to_all | solution.py:57
  56.4 0.0 copy-done
  56.4 4.1 %fusion.10 = f32[512,2240]{0,1:T(8,128)} fusion(f32[4,2240]{1,0:T(4,128)S(1)} %copy-done, s32[512]{0:T(512)S(1)} %add_select_fusion), kind=kOutput, calls=%fused_computation.19 | convolution fusion | flops 55052288 | bytes 4625408 | tf_op jit(solution)/shard_map/dot_general | solution.py:54
  60.5 8.8 %all-to-all-done = bf16[4,512,224]{1,2,0:T(8,128)(2,1)S(1)} async-done(((bf16[4,512,224]{1,2,0:T(8,128)(2,1)}), bf16[4,512,224]{1,2,0:T(8,128)(2,1)S(1)}, u32[]{:S(2)}, u32[]{:S(2)}) %all-to-all-start) | async-done | bytes 917536 | tf_op jit(solution)/shard_map/all_to_all | solution.py:57
  69.4 29.2 %all-gather.3.cloned.1.call-done = bf16[896,2240]{1,0:T(8,128)(2,1)} async-done(((bf16[224,2240]{1,0:T(8,128)(2,1)}), bf16[896,2240]{1,0:T(8,128)(2,1)}) %all-gather.3.cloned.1.call-update) | async-done | bytes 4014096 | tf_op jit(solution)/shard_map/all_gather | solution.py:60
  98.6 0.0 copy-done.2
  98.6 7.8 %fusion.1 = bf16[512,2240]{0,1:T(8,128)(2,1)} fusion(f32[512,2240]{0,1:T(8,128)} %fusion.10, bf16[512,896]{0,1:T(8,128)(2,1)S(1)} %bitcast.30, bf16[896,2240]{1,0:T(8,128)(2,1)} %all-gather.3.cloned.1.call-done, bf16[512,2240]{0,1:T(8,128)(2,1)S(1)} %copy-done.2), kind=kOutput, calls=%fused_computation.2 | convolution fusion | flops 2059796480 | bytes 14106624 | tf_op jit(solution)/shard_map/dot_general | solution.py:58
  (3 shorter events, 0.0 us)
Async XLA Ops:
  6.5 49.9 %copy-start = (f32[4,2240]{1,0:T(4,128)S(1)}, f32[4,2240]{1,0:T(4,128)}, u32[]{:S(2)}) copy-start(f32[4,2240]{1,0:T(4,128)} %param.11) | copy-start | bytes 107524
  6.5 7.4 %copy-start.1 = (bf16[2048,224]{0,1:T(8,128)(2,1)S(1)}, bf16[2048,224]{0,1:T(8,128)(2,1)}, u32[]{:S(2)}) copy-start(bf16[2048,224]{0,1:T(8,128)(2,1)} %param.7) | copy-start | bytes 2752516
  6.5 92.0 %all-gather.3.cloned.1.call-start = ((), (), s32[]{:S(2)}) async-start(), calls=%async_computation.1 | async-start | bytes 5160960 | tf_op jit(solution)/shard_map/all_gather | solution.py:60
  52.7 45.9 %copy-start.2 = (bf16[512,2240]{0,1:T(8,128)(2,1)S(1)}, bf16[512,2240]{0,1:T(8,128)(2,1)}, u32[]{:S(2)}) copy-start(bf16[512,2240]{0,1:T(8,128)(2,1)} %param.9) | copy-start | bytes 6881284
  52.7 16.6 %all-to-all-start = ((bf16[4,512,224]{1,2,0:T(8,128)(2,1)}), bf16[4,512,224]{1,2,0:T(8,128)(2,1)S(1)}, u32[]{:S(2)}, u32[]{:S(2)}) async-start(bf16[4,512,224]{1,2,0:T(8,128)(2,1)} %bitcast.5), calls=%async_computation | async-start | bytes 1835008 | tf_op jit(solution)/shard_map/all_to_all | solution.py:57
Sparse Core Ops, SparseCore 0:
  8.9 89.6 all-gather.2
where the time goes:
time: 114 us; the launch traced here: 113 us
  waiting for transfers between devices  38.8 us (34%)
  blocking collectives  33.1 us (29%)
  matrix products  15.5 us (14%)
  between operations  13.5 us (12%)
  local copies, waits for them, and re-layouts  4.76 us (4%)
  other arithmetic  3.95 us (3%)
  starting transfers between devices  3.64 us (3%)
    all_gather x1, waiting for transfers between devices, per_device(): lax.all_gather(out_proj, 'frames', axis=0, tiled=True)  29.2 us
    all_gather x1, blocking collectives, per_device(): lax.all_gather(own_state[None], 'frames', axis=0, tiled=True)  19.9 us
    all_gather x1, blocking collectives, per_device(): lax.all_gather(own_sum[None], 'frames', axis=0, tiled=True)  13.3 us
    all_to_all x1, waiting for transfers between devices, per_device(): lax.all_to_all(attended, 'heads', split_axis=0, concat_axis=1, tiled=True)  8.84 us
    dot_general x1, matrix products, per_device(): jnp.dot(token_rows, lax.all_gather(out_proj, 'frames', axis=0, tiled=True...  7.75 us
    dot_general x1, matrix products, per_device(): jnp.dot(selector, frame_gate, precision=lax.Precision.HIGHEST, preferred_...  4.13 us
    all_to_all x1, starting transfers between devices, per_device(): lax.all_to_all(attended, 'heads', split_axis=0, concat_axis=1, tiled=True)  3.64 us
    reshape x1, local copies, waits for them, and re-layouts, per_device(): value_frames = value_heads.reshape(block_shape)  3.23 us
  transfers between devices with their start and end apart: 2, of which 2 were waited for; matrix products, arithmetic and copies ran while one was open for 14% of the time, Pallas kernels for 0%

commit v1 on v0

--- a/solution.py
+++ b/solution.py
@@ -1,3 +1,4 @@
+import functools
 import jax
 import jax.numpy as jnp
 from jax import lax
@@ -7,6 +8,31 @@
 HEADS_DEV = 2
 FRAME_TOK = 512
 EPSILON = 1e-06
+
+
+def pass_pipes(local_array, on_dim):
+    part_now = list(local_array.shape[1:])
+    part_now[on_dim] *= local_array.shape[0]
+    return jnp.moveaxis(local_array, 0, on_dim).reshape(part_now)
+
+
+def _meet_stops_all(w_in, dev_axis):
+    shares = lax.axis_size(dev_axis)
+    current_block = w_in[None]
+    for hop_no in range(shares.bit_length() - 1):
+        carry = 1 << hop_no
+        w2 = lax.ppermute(current_block, dev_axis, [(d, d ^ carry) for d in range(shares)])
+        last = jnp.stack([current_block, w2])
+        mixed_arr = lax.axis_index(dev_axis) >> hop_no & 1
+        current_block = jnp.where(mixed_arr == 0, last, last[::-1]).reshape(-1, *w_in.shape)
+    return current_block
+
+
+def roots_shape(x_in, base_x, join_dim):
+    return pass_pipes(_meet_stops_all(x_in, base_x), join_dim)
+
+
+draft_members_all = functools.partial(roots_shape, base_x="frames", join_dim=0)
 
 
 def per_device(query_heads, key_heads, value_heads, residual, out_proj, frame_gate):
@@ -24,7 +50,7 @@
     own_sum = jnp.sum(frame_sum, axis=0)
     position = lax.axis_index("frames")
     gathered = (
-        lax.all_gather(own_state[None], "frames", axis=0, tiled=True),
+        draft_members_all(own_state[None]),
         lax.all_gather(own_sum[None], "frames", axis=0, tiled=True),
     )
     pieces = gathered[0].shape[0]

time: 114 us -> 116 us (1.018)
  blocking collectives: 33.1 us -> 10.5 us
  waiting for transfers between devices: 38.8 us -> 59 us
  starting transfers between devices: 3.64 us -> 9.39 us
    ppermute x0 -> x2, waiting for transfers between devices: none -> 23.3 us  [_meet_stops_all(): lax.ppermute(current_block, dev_axis, [(d, d ^ carry) for d in range(shar...]
    all_gather x1 -> x0, blocking collectives: 19.9 us -> none  [per_device(): lax.all_gather(own_state[None], 'frames', axis=0, tiled=True)]
    ppermute x0 -> x2, starting transfers between devices: none -> 5.75 us  [_meet_stops_all(): lax.ppermute(current_block, dev_axis, [(d, d ^ carry) for d in range(shar...]
    all_gather x1, waiting for transfers between devices: 29.2 us -> 26.1 us  [per_device(): lax.all_gather(out_proj, 'frames', axis=0, tiled=True)]
    all_gather x1, blocking collectives: 13.3 us -> 10.5 us  [per_device(): lax.all_gather(own_sum[None], 'frames', axis=0, tiled=True)]
    max x1, other arithmetic: 1.24 us -> 0.06 us  [per_device(): query_pos = jnp.maximum(query_heads, 0).reshape(block_shape)]
    reduce_sum x1, other arithmetic: 1.44 us -> 0.26 us  [per_device(): own_sum = jnp.sum(frame_sum, axis=0)]
    max x1, other arithmetic: 0.06 us -> 1.24 us  [per_device(): key_pos = jnp.maximum(key_heads, 0).reshape(block_shape)]
  transfers between devices with their start and end apart: 2 -> 4, of which waited for: 2 -> 3; matrix products, arithmetic and copies ran while one was open for 14% -> 13% of each run, Pallas kernels for 0% -> 0%
where the time goes in v1:
time: 116 us
  waiting for transfers between devices  59 us (51%)
  matrix products  15.5 us (13%)
  between operations  13.5 us (12%)
  blocking collectives  10.5 us (9%)
  starting transfers between devices  9.39 us (8%)
  local copies, waits for them, and re-layouts  4.85 us (4%)
  other arithmetic  2.87 us (2%)
    all_gather x1, waiting for transfers between devices, per_device(): lax.all_gather(out_proj, 'frames', axis=0, tiled=True)  26.1 us
    ppermute x2, waiting for transfers between devices, _meet_stops_all(): lax.ppermute(current_block, dev_axis, [(d, d ^ carry) for d in range(shar...  23.3 us
    all_gather x1, blocking collectives, per_device(): lax.all_gather(own_sum[None], 'frames', axis=0, tiled=True)  10.5 us
    all_to_all x1, waiting for transfers between devices, per_device(): lax.all_to_all(attended, 'heads', split_axis=0, concat_axis=1, tiled=True)  8.83 us
    dot_general x1, matrix products, per_device(): jnp.dot(token_rows, lax.all_gather(out_proj, 'frames', axis=0, tiled=True...  7.75 us
    ppermute x2, starting transfers between devices, _meet_stops_all(): lax.ppermute(current_block, dev_axis, [(d, d ^ carry) for d in range(shar...  5.75 us
    dot_general x1, matrix products, per_device(): jnp.dot(selector, frame_gate, precision=lax.Precision.HIGHEST, preferred_...  4.13 us
    all_to_all x1, starting transfers between devices, per_device(): lax.all_to_all(attended, 'heads', split_axis=0, concat_axis=1, tiled=True)  3.64 us
  transfers between devices with their start and end apart: 4, of which 3 were waited for; matrix products, arithmetic and copies ran while one was open for 13% of the time, Pallas kernels for 0%

profile of v1, /device:TPU:0, one launch (start us, length us, event | category | flops | bytes accessed | tf_op | source)
XLA Modules:
  0.0 115.7 jit_solution(16806402217301887596)
XLA Ops:
  6.5 0.0 copy-start
  6.5 0.0 all-gather.2.cloned.1.call-start
  6.5 0.7 all-gather.2.cloned.1.call-update
  7.3 0.0 copy-start.1
  7.3 3.3 %reshape.52 = bf16[4,512,2,112]{1,0,3,2:T(4,128)(2,1)} reshape(bf16[2048,224]{0,1:T(8,128)(2,1)} %param.8) | data formatting | bytes 1835008 | tf_op jit(solution)/shard_map/reshape | solution.py:44
  10.6 1.2 %broadcast_maximum_fusion.1 = bf16[2048,224]{0,1:T(8,128)(2,1)S(1)} fusion(bf16[2048,224]{0,1:T(8,128)(2,1)} %param.7), kind=kLoop, calls=%fused_computation.20 | loop fusion | flops 458752 | bytes 1835008 | tf_op jit(solution)/shard_map/max | solution.py:43
  11.8 0.7 reshape.51
  12.5 0.0 copy-start.2
  12.5 1.9 %fusion.21 = (f32[2,112,112]{2,1,0:T(8,128)S(1)}, f32[4,2,112,112]{3,2,1,0:T(8,128)S(1)}) fusion(bf16[4,512,2,112]{1,0,3,2:T(4,128)(2,1)} %reshape.52, bf16[4,512,2,112]{1,0,3,2:T(4,128)(2,1)S(1)} %reshape.51), kind=kOutput, calls=%fused_computation.44 | convolution fusion | flops 102835712 | bytes 2336768 | tf_op jit(solution)/shard_map/fthi,fthj->fhij/dot_general | solution.py:45
  14.4 3.1 %collective-permute-start = (f32[1,1,2,112,112]{4,3,2,1,0:T(8,128)S(1)}, f32[1,1,2,112,112]{4,3,2,1,0:T(8,128)S(1)}, u32[]{:S(2)}, u32[]{:S(2)}) collective-permute-start(f32[1,1,2,112,112]{4,3,2,1,0:T(8,128)S(1)} %bitcast.42), channel_id=1, source_target_pairs={{0,4},{4,0},{8,12},{12,8},{1,5},{5,1},{9,13},{13,9},{2,6},{6,2},{1... | collective-permute-start | bytes 301064 | tf_op jit(solution)/shard_map/ppermute | solution.py:24
  17.5 0.0 copy-done.1
  17.5 0.3 convert_reduce_fusion.1
  17.8 0.1 broadcast_in_dim.37
  17.9 0.0 copy-done.2
  17.9 0.1 broadcast_maximum_fusion
  17.9 0.7 reshape.54
  18.6 0.4 convert_reduce_fusion
  19.0 0.4 reduce_window_sum.23
  19.4 10.5 %all_gather.6 = f32[4,2,112]{2,1,0:T(2,128)S(1)} all-gather(f32[1,2,112]{2,1,0:T(2,128)S(1)} %broadcast_in_dim.37), channel_id=1, replica_groups=mesh['groups'=2,'frames'=4,'heads'=4] {'frames'}, dimensions={0}, use_global_device_ids=true | all-gather | bytes 4480 | tf_op jit(solution)/shard_map/all_gather | solution.py:54
  30.0 0.1 select_reduce_fusion
  30.1 0.1 fusion.16
  30.2 0.1 copy.26
  30.3 0.4 fusion.7
  30.7 0.0 collective-permute-done
  30.7 2.6 %collective-permute-start.1 = (f32[2,1,2,112,112]{4,3,2,0,1:T(8,128)S(1)}, f32[2,1,2,112,112]{4,3,2,0,1:T(8,128)S(1)}, u32[]{:S(2)}, u32[]{:S(2)}) collective-permute-start(f32[2,1,2,112,112]{4,3,2,0,1:T(8,128)S(1)} %get-tuple-element.6), channel_id=1, source_target_pairs={{0,8},{4,12},{8,0},{12,4},{1,9},{5,13},{9,1},{13,5},{2,10},{6,14},... | collective-permute-start | bytes 602120 | tf_op jit(solution)/shard_map/ppermute | solution.py:24
  33.4 23.3 %collective-permute-done.1 = f32[2,1,2,112,112]{4,3,2,0,1:T(8,128)S(1)} collective-permute-done((f32[2,1,2,112,112]{4,3,2,0,1:T(8,128)S(1)}, f32[2,1,2,112,112]{4,3,2,0,1:T(8,128)S(1)}, u32[]{:S(2)}, u32[]{:S(2)}) %collective-permute-start.1) | collective-permute-done | bytes 200736 | tf_op jit(solution)/shard_map/ppermute | solution.py:24
  56.7 0.1 fusion.11
  56.9 0.1 fusion.3
  56.9 1.4 %fusion.2 = bf16[4,512,2,112]{1,3,2,0:T(8,128)(2,1)} fusion(bf16[4,2,112,112]{3,2,1,0:T(8,128)(2,1)S(1)} %fusion.3, f32[4,512,2]{1,2,0:T(2,128)S(1)} %fusion.17, bf16[4,512,2,112]{1,0,3,2:T(4,128)(2,1)S(1)} %reshape.54), kind=kOutput, calls=%fused_computation.4 | convolution fusion | flops 103677952 | bytes 2052096 | tf_op jit(solution)/shard_map/fthi,fhij->fthj/dot_general | solution.py:64
  58.3 0.0 copy-start.3
  58.3 3.6 %all-to-all-start = ((bf16[4,512,224]{1,2,0:T(8,128)(2,1)}), bf16[4,512,224]{1,2,0:T(8,128)(2,1)S(1)}, u32[]{:S(2)}, u32[]{:S(2)}) async-start(bf16[4,512,224]{1,2,0:T(8,128)(2,1)} %bitcast.12), calls=%async_computation | async-start | bytes 1835008 | tf_op jit(solution)/shard_map/all_to_all | solution.py:83
  62.0 0.0 copy-done
  62.0 4.1 %fusion.12 = f32[512,2240]{0,1:T(8,128)} fusion(f32[4,2240]{1,0:T(4,128)S(1)} %copy-done, s32[512]{0:T(512)S(1)} %add_select_fusion), kind=kOutput, calls=%fused_computation.23 | convolution fusion | flops 55052288 | bytes 4625408 | tf_op jit(solution)/shard_map/dot_general | solution.py:80
  66.1 8.8 %all-to-all-done = bf16[4,512,224]{1,2,0:T(8,128)(2,1)S(1)} async-done(((bf16[4,512,224]{1,2,0:T(8,128)(2,1)}), bf16[4,512,224]{1,2,0:T(8,128)(2,1)S(1)}, u32[]{:S(2)}, u32[]{:S(2)}) %all-to-all-start) | async-done | bytes 917536 | tf_op jit(solution)/shard_map/all_to_all | solution.py:83
  75.0 26.1 %all-gather.2.cloned.1.call-done = bf16[896,2240]{1,0:T(8,128)(2,1)} async-done(((bf16[224,2240]{1,0:T(8,128)(2,1)}), bf16[896,2240]{1,0:T(8,128)(2,1)}) %all-gather.2.cloned.1.call-update) | async-done | bytes 4014096 | tf_op jit(solution)/shard_map/all_gather | solution.py:86
  101.1 0.0 copy-done.3
  101.1 7.8 %fusion.1 = bf16[512,2240]{0,1:T(8,128)(2,1)} fusion(f32[512,2240]{0,1:T(8,128)} %fusion.12, bf16[512,896]{0,1:T(8,128)(2,1)S(1)} %bitcast.40, bf16[896,2240]{1,0:T(8,128)(2,1)} %all-gather.2.cloned.1.call-done, bf16[512,2240]{0,1:T(8,128)(2,1)S(1)} %copy-done.3), kind=kOutput, calls=%fused_computation.2 | convolution fusion | flops 2059796480 | bytes 14106624 | tf_op jit(solution)/shard_map/dot_general | solution.py:84
  (7 shorter events, 0.1 us)
Async XLA Ops:
  6.5 55.5 %copy-start = (f32[4,2240]{1,0:T(4,128)S(1)}, f32[4,2240]{1,0:T(4,128)}, u32[]{:S(2)}) copy-start(f32[4,2240]{1,0:T(4,128)} %param.11) | copy-start | bytes 107524
  6.5 94.5 %all-gather.2.cloned.1.call-start = ((), (), s32[]{:S(2)}) async-start(), calls=%async_computation.1 | async-start | bytes 5160960 | tf_op jit(solution)/shard_map/all_gather | solution.py:86
  7.3 10.3 %copy-start.1 = (bf16[2048,224]{0,1:T(8,128)(2,1)S(1)}, bf16[2048,224]{0,1:T(8,128)(2,1)}, u32[]{:S(2)}) copy-start(bf16[2048,224]{0,1:T(8,128)(2,1)} %param.7) | copy-start | bytes 2752516
  12.5 5.4 %copy-start.2 = (bf16[2048,224]{0,1:T(8,128)(2,1)S(1)}, bf16[2048,224]{0,1:T(8,128)(2,1)}, u32[]{:S(2)}) copy-start(bf16[2048,224]{0,1:T(8,128)(2,1)} %param.6) | copy-start | bytes 2752516
  14.4 16.3 %collective-permute-start = (f32[1,1,2,112,112]{4,3,2,1,0:T(8,128)S(1)}, f32[1,1,2,112,112]{4,3,2,1,0:T(8,128)S(1)}, u32[]{:S(2)}, u32[]{:S(2)}) collective-permute-start(f32[1,1,2,112,112]{4,3,2,1,0:T(8,128)S(1)} %bitcast.42), channel_id=1, source_target_pairs={{0,4},{4,0},{8,12},{12,8},{1,5},{5,1},{9,13},{13,9},{2,6},{6,2},{1... | collective-permute-start | bytes 301064 | tf_op jit(solution)/shard_map/ppermute | solution.py:24
  30.7 26.0 %collective-permute-start.1 = (f32[2,1,2,112,112]{4,3,2,0,1:T(8,128)S(1)}, f32[2,1,2,112,112]{4,3,2,0,1:T(8,128)S(1)}, u32[]{:S(2)}, u32[]{:S(2)}) collective-permute-start(f32[2,1,2,112,112]{4,3,2,0,1:T(8,128)S(1)} %get-tuple-element.6), channel_id=1, source_target_pairs={{0,8},{4,12},{8,0},{12,4},{1,9},{5,13},{9,1},{13,5},{2,10},{6,14},... | collective-permute-start | bytes 602120 | tf_op jit(solution)/shard_map/ppermute | solution.py:24
  58.3 42.8 %copy-start.3 = (bf16[512,2240]{0,1:T(8,128)(2,1)S(1)}, bf16[512,2240]{0,1:T(8,128)(2,1)}, u32[]{:S(2)}) copy-start(bf16[512,2240]{0,1:T(8,128)(2,1)} %param.9) | copy-start | bytes 6881284
  58.3 16.6 %all-to-all-start = ((bf16[4,512,224]{1,2,0:T(8,128)(2,1)}), bf16[4,512,224]{1,2,0:T(8,128)(2,1)S(1)}, u32[]{:S(2)}, u32[]{:S(2)}) async-start(bf16[4,512,224]{1,2,0:T(8,128)(2,1)} %bitcast.12), calls=%async_computation | async-start | bytes 1835008 | tf_op jit(solution)/shard_map/all_to_all | solution.py:83
Sparse Core Ops, SparseCore 0:
  8.9 92.1 all-gather.1
